TPU v7x, 32 devices: a whole 2x2x4 slice. The times are simulated.
32 devices in a mesh: basin: 8 (over z, y), band: 4 (over x, core).
Axes of the slice: x: 2, y: 2, z: 4, core: 2. Of those that a mesh axis runs over, the one named last changes fastest.
Arguments:
- precip: float32 [6144, 8, 128], P(('basin', 'band')), may hold values from 0.002 to 0.02
- soil_water: float32 [6144, 128], P(('basin', 'band')), may hold values from 0.1 to 1
- capacity: float32 [6144, 128], P(('basin', 'band')), may hold values from 0.1 to 1
- evap_rate: float32 [6144, 128], P(('basin', 'band')), may hold values from 0.01 to 0.1
- tile_dest: int32 [6144], P(('basin', 'band')), may hold values from 0 to 31, as said below
- tile_block: int32 [6144], P(('basin', 'band')), may hold values from 0 to 7
- trib_op: float32 [256, 128, 128], P(('basin', 'band')), may hold values from 0 to 1
- trib_keep: float32 [256, 128], P(('basin', 'band')), may hold values from 0.01 to 0.6
- trib_prev: float32 [256, 128], P(('basin', 'band')), may hold values from 0 to 0.5
- trib_river: int32 [256], P(('basin', 'band')), may hold values from 0 to 3, as said below
- trib_reach: int32 [256], P(('basin', 'band')), may hold values from 0 to 127
- main_op: float32 [4, 8, 128, 128], P('band', 'basin'), may hold values from 0 to 1
- main_keep: float32 [4, 8, 128], P('band', 'basin'), may hold values from 0.002 to 0.1
- main_prev: float32 [4, 8, 128], P('band', 'basin'), may hold values from 0 to 4
- head_inflow: float32 [4, 8], P('band'), may hold values from 0.5 to 2
Outputs:
- soil_final: float32 [6144, 128], P(('basin', 'band'))
- trib_final: float32 [256, 128], P(('basin', 'band'))
- main_flow: float32 [4, 8, 8, 128], P('band', 'basin')
Inputs may be any that keep to these rules, and one draw needn't show every extreme that they name: `tile_dest`: among the 192 tiles of one device, at most 12 name the same owner. `trib_river`: among the 8 tributary blocks of one device, at most 4 name the same river.
All inputs are finite; a program needn't handle non-finite values.
Results may differ from a plain program's by a relative error of at most 0.00016.
Values sent between devices are 32-bit elements; how exact they have to be, the bound alone decides.
No kernel may reach another device: no remote copies, remote signals or barrier semaphores. Data moves between devices by JAX's collectives and lax.ppermute only.
A program may use at most 64 MiB of HBM per device.

v0:
```python
import jax
import jax.numpy as jnp
from jax import lax
from jax.sharding import PartitionSpec as P


def entering(value, axis, join, neutral):
    count, mine = (lax.axis_size(axis), lax.axis_index(axis))
    pieces = jax.tree.map(lambda part: lax.all_gather(part, axis), value)
    running = jax.tree.map(
        lambda part, zero: jnp.full_like(part, 0) + jnp.asarray(zero, part.dtype), value, neutral
    )

    def turn(position, running):
        longer = join(running, jax.tree.map(lambda part: part[position], pieces))
        return jax.tree.map(lambda new, old: jnp.where(position < mine, new, old), longer, running)

    return lax.fori_loop(0, count - 1, turn, running)


def land_update(precip, soil_water, capacity, evap_rate):
    water = soil_water
    runoff_steps = []
    for sub_step in range(precip.shape[1]):
        rain_now = precip[:, sub_step]
        runoff_now = rain_now * water / (water + capacity)
        water = (1.0 - evap_rate) * water + rain_now - runoff_now
        runoff_steps.append(runoff_now)
    return (jnp.stack(runoff_steps, axis=1), water)


def route_series(mixed, keep, previous):
    flow = previous
    flows = []
    for sub_step in range(mixed.shape[-2]):
        flow = keep * flow + (1.0 - keep) * mixed[..., sub_step, :]
        flows.append(flow)
    return jnp.stack(flows, axis=-2)


def pack_slots(values, labels, targets, peer_count, slot_cap):
    entries = targets.shape[0]
    position = jnp.arange(entries, dtype=jnp.int32)
    earlier = (targets[:, None] == targets[None, :]) & (position[None, :] < position[:, None])
    ranking = jnp.sum(earlier.astype(jnp.int32), axis=1)
    target_slot = targets * slot_cap + ranking
    buffer = (
        jnp.zeros((peer_count * slot_cap, values.shape[1]), values.dtype)
        .at[target_slot]
        .set(values)
    )
    slot_labels = jnp.zeros((peer_count * slot_cap,), jnp.int32).at[target_slot].set(labels)
    return (buffer, slot_labels)


def compose(earlier, later):
    new_map = jnp.dot(later[0], earlier[0], precision=lax.Precision.HIGHEST)
    new_shift = jnp.dot(later[0], earlier[1], precision=lax.Precision.HIGHEST) + later[1]
    return (new_map, new_shift)


def local(
    precip,
    soil_water,
    capacity,
    evap_rate,
    tile_dest,
    tile_block,
    trib_op,
    trib_keep,
    trib_prev,
    trib_river,
    trib_reach,
    main_op,
    main_keep,
    main_prev,
    head_inflow,
):
    tile_count = precip.shape[0]
    sub_steps = precip.shape[1]
    reaches = precip.shape[2]
    blocks = trib_op.shape[0]
    chains = lax.axis_size("basin")
    rivers = lax.axis_size("band")
    shards = chains * rivers
    operator = main_op[0, 0]
    keep_main = main_keep[0, 0]
    decay = keep_main[reaches - 1]
    through = operator[reaches - 1, 0]
    transfer = jnp.zeros((sub_steps, sub_steps), jnp.float32)
    power = jnp.ones((), jnp.float32)
    for lag in range(sub_steps):
        transfer = transfer + power * jnp.eye(sub_steps, k=-lag, dtype=jnp.float32)
        power = power * decay
    transfer = transfer * (through * (1.0 - decay))
    runoff, water = land_update(precip, soil_water, capacity, evap_rate)
    tile_cap = max(2, 2 * tile_count // shards)
    buffer, slot_labels = pack_slots(
        runoff.reshape(tile_count, sub_steps * reaches), tile_block, tile_dest, shards, tile_cap
    )
    buffer = buffer.reshape(chains, rivers, tile_cap, sub_steps * reaches)
    slot_labels = slot_labels.reshape(chains, rivers, tile_cap)
    arrived, arrived_ids = (
        lax.all_to_all(
            lax.all_to_all(buffer, "basin", split_axis=0, concat_axis=0, tiled=True),
            "band",
            split_axis=1,
            concat_axis=1,
            tiled=True,
        ),
        lax.all_to_all(
            lax.all_to_all(slot_labels, "basin", split_axis=0, concat_axis=0, tiled=True),
            "band",
            split_axis=1,
            concat_axis=1,
            tiled=True,
        ),
    )
    received = arrived.reshape(-1, sub_steps * reaches)
    block_pick = (
        arrived_ids.reshape(-1)[:, None] == jnp.arange(blocks, dtype=jnp.int32)[None, :]
    ).astype(jnp.float32)
    lateral = jnp.einsum("sk,sx->kx", block_pick, received, precision=lax.Precision.HIGHEST)
    trib_mixed = jnp.einsum(
        "brc,btc->btr",
        trib_op,
        lateral.reshape(blocks, sub_steps, reaches),
        precision=lax.Precision.HIGHEST,
    )
    trib_flows = route_series(trib_mixed, trib_keep, trib_prev)
    outlet = trib_flows[:, :, reaches - 1]
    branch_cap = max(2, 2 * blocks // rivers)
    sent, sent_reach = pack_slots(outlet, trib_reach, trib_river, rivers, branch_cap)
    got, got_reach = (
        lax.all_to_all(
            sent.reshape(rivers, branch_cap, sub_steps),
            "band",
            split_axis=0,
            concat_axis=0,
            tiled=True,
        ),
        lax.all_to_all(
            sent_reach.reshape(rivers, branch_cap), "band", split_axis=0, concat_axis=0, tiled=True
        ),
    )
    reach_pick = (
        got_reach.reshape(-1)[:, None] == jnp.arange(reaches, dtype=jnp.int32)[None, :]
    ).astype(jnp.float32)
    branch_in = jnp.einsum(
        "sr,st->tr", reach_pick, got.reshape(-1, sub_steps), precision=lax.Precision.HIGHEST
    )
    main_mixed = jnp.einsum("rc,tc->tr", operator, branch_in, precision=lax.Precision.HIGHEST)
    base_flows = route_series(main_mixed, keep_main, main_prev[0, 0])
    own_exit = base_flows[:, reaches - 1]
    unit_map = jnp.eye(sub_steps, dtype=jnp.float32)
    no_shift = jnp.zeros((sub_steps,), jnp.float32)
    prefix_map, prefix_shift = entering(
        (transfer, own_exit), "basin", compose, (unit_map, no_shift)
    )
    entry = jnp.dot(prefix_map, head_inflow[0], precision=lax.Precision.HIGHEST) + prefix_shift
    fed_mixed = main_mixed + entry[:, None] * operator[:, 0][None, :]
    main_flows = route_series(fed_mixed, keep_main, main_prev[0, 0])
    return (water, trib_flows[:, sub_steps - 1], main_flows[None, None])


def solution(mesh):
    return jax.shard_map(
        local,
        mesh=mesh,
        in_specs=(
            P(("basin", "band"), None, None),
            P(("basin", "band"), None),
            P(("basin", "band"), None),
            P(("basin", "band"), None),
            P(("basin", "band")),
            P(("basin", "band")),
            P(("basin", "band"), None, None),
            P(("basin", "band"), None),
            P(("basin", "band"), None),
            P(("basin", "band")),
            P(("basin", "band")),
            P("band", "basin", None, None),
            P("band", "basin", None),
            P("band", "basin", None),
            P("band", None),
        ),
        out_specs=(
            P(("basin", "band"), None),
            P(("basin", "band"), None),
            P("band", "basin", None, None),
        ),
        check_vma=False,
    )
```

profile of v0, /device:TPU:0, one launch (start us, length us, event | category | flops | bytes accessed | tf_op | source)
XLA Modules:
  0.0 160.7 jit_solution(4654353818864081058)
XLA Ops:
  0.7 0.9 convert_reduce_fusion
  1.6 0.7 compare_select_fusion
  2.3 1.3 scatter_custom_fusion
  3.7 0.7 reshape.312
  4.4 7.3 %all-to-all-start = ((s32[8,4,12]{2,1,0:T(4,128)}), s32[8,4,12]{2,1,0:T(4,128)S(1)}, u32[]{:S(2)}, u32[]{:S(2)}) async-start(s32[8,4,12]{2,1,0:T(4,128)} %reshape.312), calls=%async_computation | async-start | bytes 32768 | tf_op jit(solution)/shard_map/all_to_all | solution.py:112
  11.7 4.1 %fusion.63 = (f32[192,1,128]{2,1,0:T(1,128)S(1)}, f32[192,1,128]{2,1,0:T(1,128)S(1)}, f32[192,1,128]{2,1,0:T(1,128)S(1)}, f32[192,1,128]{2,1,0:T(1,128)S(1)}, f3...) fusion(f32[192,8,128]{2,1,0:T(8,128)} %param.17), kind=kLoop, calls=%fused_computation.144 | loop fusion | bytes 1572864 | tf_op jit(solution)/shard_map/slice | solution.py:25
  16.0 0.1 bitcast_dynamic-update-slice_fusion.4
  16.4 2.5 %scatter_custom_fusion.1 = f32[384,1024]{1,0:T(8,128)} fusion(s32[192]{0:T(256)S(1)} %compare_select_fusion, f32[8,24,8,128]{3,2,1,0:T(8,128)S(1)} %bitcast.264, f32[]{:T(128)} %constant.60.clone.1), kind=kCustom, calls=%fused_computation.20 | custom fusion | bytes 2359300 | tf_op jit(solution)/shard_map/scatter | solution.py:50
  18.9 1.4 reshape.314
  20.3 2.2 %copy.110 = f32[8,4,12,1024]{3,1,2,0:T(4,128)} copy(f32[8,4,12,1024]{3,2,1,0:T(8,128)S(1)} %reshape.314) | data formatting | bytes 3145728 | tf_op jit(solution)/shard_map/reshape | solution.py:101
  22.5 6.1 %all-to-all-start.2 = ((f32[8,4,12,1024]{3,1,2,0:T(4,128)}), f32[8,4,12,1024]{3,1,2,0:T(4,128)S(1)}, u32[]{:S(2)}, u32[]{:S(2)}) async-start(f32[8,4,12,1024]{3,1,2,0:T(4,128)} %copy.110), calls=%async_computation.2 | async-start | bytes 3145728 | tf_op jit(solution)/shard_map/all_to_all | solution.py:105
  28.7 0.6 copy.107
  29.3 35.8 %all-to-all-done.2 = f32[8,4,12,1024]{3,1,2,0:T(4,128)S(1)} async-done(((f32[8,4,12,1024]{3,1,2,0:T(4,128)}), f32[8,4,12,1024]{3,1,2,0:T(4,128)S(1)}, u32[]{:S(2)}, u32[]{:S(2)}) %all-to-all-start.2) | async-done | bytes 1572896 | tf_op jit(solution)/shard_map/all_to_all | solution.py:105
  65.1 3.3 %all-to-all-start.1 = ((s32[8,4,12]{2,0,1:T(8,128)}), s32[8,4,12]{2,0,1:T(8,128)S(1)}, u32[]{:S(2)}, u32[]{:S(2)}) async-start(s32[8,4,12]{2,0,1:T(8,128)} %copy.107), calls=%async_computation.1 | async-start | bytes 32768 | tf_op jit(solution)/shard_map/all_to_all | solution.py:111
  68.4 0.2 convert_reduce_fusion.1
  68.6 2.1 %copy.111 = f32[8,4,12,1024]{3,0,2,1:T(8,128)} copy(f32[8,4,12,1024]{3,1,2,0:T(4,128)S(1)} %all-to-all-done.2) | data formatting | bytes 3145728 | tf_op jit(solution)/shard_map/all_to_all | solution.py:105
  70.6 1.5 all-to-all-done.1
  72.2 3.6 %all-to-all-start.3 = ((f32[8,4,12,1024]{3,0,2,1:T(8,128)}), f32[8,4,12,1024]{3,0,2,1:T(8,128)S(1)}, u32[]{:S(2)}, u32[]{:S(2)}) async-start(f32[8,4,12,1024]{3,0,2,1:T(8,128)} %copy.111), calls=%async_computation.3 | async-start | bytes 3145728 | tf_op jit(solution)/shard_map/all_to_all | solution.py:104
  75.8 0.7 scatter_custom_fusion.3
  76.5 0.7 all_to_all.26
  77.2 0.5 slice.158
  77.7 0.6 slice.129
  84.2 0.7 add_multiply_fusion
  84.9 30.4 %all_gather.7 = f32[8,8,8]{2,1,0:T(8,128)S(1)} all-gather(f32[1,8,8]{2,1,0:T(8,128)S(1)} %add_multiply_fusion), channel_id=1, replica_groups=mesh['basin'=8,'band'=4] {'basin'}, dimensions={0}, use_global_device_ids=true | all-gather | bytes 2304 | tf_op jit(solution)/shard_map/all_gather | solution.py:9
  115.3 0.1 slice_reduce_fusion
  115.4 0.7 add_subtract_fusion
  116.1 0.1 eq.142
  116.3 1.2 copy-done.2
  117.4 3.2 %all-to-all-start.5 = ((s32[4,1,4]{2,1,0:T(1,128)}), s32[4,1,4]{2,1,0:T(1,128)S(1)}, u32[]{:S(2)}, u32[]{:S(2)}) async-start(s32[4,1,4]{2,1,0:T(1,128)} %bitcast.40), calls=%async_computation.5 | async-start | bytes 4096 | tf_op jit(solution)/shard_map/all_to_all | solution.py:142
  120.7 2.4 %copy.112 = f32[8,4,12,1024]{3,2,1,0:T(8,128)S(1)} copy(f32[8,4,12,1024]{3,0,2,1:T(8,128)} %copy-done.2) | data formatting | bytes 3145728 | tf_op jit(solution)/shard_map/all_to_all | solution.py:104
  123.0 1.3 reshape.315
  124.4 1.9 %copy.113 = f32[1024,384]{1,0:T(8,128)S(1)} copy(f32[1024,384]{0,1:T(8,128)} %bitcast.246) | data formatting | bytes 3145728 | tf_op jit(solution)/shard_map/sk,sx->kx/dot_general | solution.py:123
  126.3 0.8 fusion.20
  127.1 0.9 fusion.17
  128.2 0.6 constant_dynamic-update-slice_fusion
  128.9 0.1 copy.122
  129.0 1.2 scatter_custom_fusion.2
  130.2 3.3 %all-to-all-start.4 = ((f32[4,4,8]{2,1,0:T(4,128)}), f32[4,4,8]{2,1,0:T(4,128)S(1)}, u32[]{:S(2)}, u32[]{:S(2)}) async-start(f32[4,4,8]{2,1,0:T(4,128)} %bitcast.38), calls=%async_computation.4 | async-start | bytes 16384 | tf_op jit(solution)/shard_map/all_to_all | solution.py:135
  133.5 0.6 dynamic-slice
  134.7 0.5 broadcast.431
  135.2 0.7 reduce.7
  136.0 1.3 all-to-all-done.4
  137.3 0.2 fusion.22
  137.5 0.2 fusion.49
  137.8 0.2 slice_reduce_fusion.1
  138.0 0.2 dynamic-update-slice
  138.2 19.5 %all-reduce = f32[64]{0:T(128)S(1)} all-reduce(f32[64]{0:T(128)S(1)} %dynamic-update-slice), channel_id=2, replica_groups=mesh['basin'=8,'band'=4] {'basin'}, use_global_device_ids=true, to_apply=%add | all-reduce | flops 64 | bytes 512
  157.8 2.0 %while.16 = (s32[]{:T(128)}, f32[8,8]{1,0:T(8,128)S(1)}, f32[8]{0:T(128)S(1)}, s32[]{:T(128)}, f32[8,8,8]{2,1,0:T(8,128)S(1)}, /*index=5*/f32[8,8]{1,0:T(8,128)S(1)}, s32[]{:T(128)}, s32[]{:T(128)}) while((s32[]{:T(128)}, f32[8,8]{1,0:T(8,128)S(1)}, f32[8]{0:T(128)S(1)}, s32[]{:T(128)}, f32[8,8,8]{2,1,0:T(8,128)S(1)}, ...), condition=%wide.region_7.8_spmd.clone, body=%wide.region_6.7_spmd.clone.sunk | while | flops 7012 | bytes 21460 | solution.py:18
  157.8 0.1 convolution_select_fusion.2
  157.9 0.1 fusion.80
  158.0 0.1 convolution_select_fusion.2
  158.2 0.1 fusion.80
  158.3 0.1 convolution_select_fusion.2
  158.5 0.1 fusion.80
  158.6 0.1 convolution_select_fusion.2
  158.8 0.1 fusion.80
  158.9 0.1 convolution_select_fusion.2
  159.1 0.1 fusion.80
  159.2 0.1 convolution_select_fusion.2
  159.4 0.1 fusion.80
  159.5 0.1 convolution_select_fusion.2
  159.6 0.1 fusion.80
  159.8 0.1 fusion.11
  160.0 0.6 stack.95
  (73 shorter events, 1.1 us)
Async XLA Ops:
  0.6 126.5 %copy-start = (f32[8,128,128]{2,1,0:T(8,128)S(1)}, f32[8,128,128]{2,1,0:T(8,128)}, u32[]{:S(2)}) copy-start(f32[8,128,128]{2,1,0:T(8,128)} %param.23) | copy-start | bytes 1572868
  0.6 15.2 %copy-start.1 = (f32[192,128]{1,0:T(8,128)S(1)}, f32[192,128]{1,0:T(8,128)}, u32[]{:S(2)}) copy-start(f32[192,128]{1,0:T(8,128)} %param.19) | copy-start | bytes 294916
  0.7 15.2 %copy-start.4 = (f32[192,128]{1,0:T(8,128)S(1)}, f32[192,128]{1,0:T(8,128)}, u32[]{:S(2)}) copy-start(f32[192,128]{1,0:T(8,128)} %param.18) | copy-start | bytes 294916
  0.7 15.2 %copy-start.3 = (f32[192,128]{1,0:T(8,128)S(1)}, f32[192,128]{1,0:T(8,128)}, u32[]{:S(2)}) copy-start(f32[192,128]{1,0:T(8,128)} %param.20) | copy-start | bytes 294916
  4.4 18.1 %all-to-all-start = ((s32[8,4,12]{2,1,0:T(4,128)}), s32[8,4,12]{2,1,0:T(4,128)S(1)}, u32[]{:S(2)}, u32[]{:S(2)}) async-start(s32[8,4,12]{2,1,0:T(4,128)} %reshape.312), calls=%async_computation | async-start | bytes 32768 | tf_op jit(solution)/shard_map/all_to_all | solution.py:112
  22.5 45.8 %copy-start.10 = (s32[8]{0:T(128)S(1)}, s32[8]{0:T(128)}, u32[]{:S(2)}) copy-start(s32[8]{0:T(128)} %param.26) | copy-start | bytes 100
  22.5 42.6 %all-to-all-start.2 = ((f32[8,4,12,1024]{3,1,2,0:T(4,128)}), f32[8,4,12,1024]{3,1,2,0:T(4,128)S(1)}, u32[]{:S(2)}, u32[]{:S(2)}) async-start(f32[8,4,12,1024]{3,1,2,0:T(4,128)} %copy.110), calls=%async_computation.2 | async-start | bytes 3145728 | tf_op jit(solution)/shard_map/all_to_all | solution.py:105
  65.1 7.1 %all-to-all-start.1 = ((s32[8,4,12]{2,0,1:T(8,128)}), s32[8,4,12]{2,0,1:T(8,128)S(1)}, u32[]{:S(2)}, u32[]{:S(2)}) async-start(s32[8,4,12]{2,0,1:T(8,128)} %copy.107), calls=%async_computation.1 | async-start | bytes 32768 | tf_op jit(solution)/shard_map/all_to_all | solution.py:111
  70.6 6.6 %copy-start.5 = (f32[1,1,128,128]{3,2,1,0:T(8,128)S(1)}, f32[1,1,128,128]{3,2,1,0:T(8,128)}, u32[]{:S(2)}) copy-start(f32[1,1,128,128]{3,2,1,0:T(8,128)} %param.28) | copy-start | bytes 196612
  70.6 7.1 %copy-start.8 = (f32[1,1,128]{2,1,0:T(1,128)S(1)}, f32[1,1,128]{2,1,0:T(1,128)}, u32[]{:S(2)}) copy-start(f32[1,1,128]{2,1,0:T(1,128)} %param.29) | copy-start | bytes 1540
  72.2 44.1 %all-to-all-start.3 = ((f32[8,4,12,1024]{3,0,2,1:T(8,128)}), f32[8,4,12,1024]{3,0,2,1:T(8,128)S(1)}, u32[]{:S(2)}, u32[]{:S(2)}) async-start(f32[8,4,12,1024]{3,0,2,1:T(8,128)} %copy.111), calls=%async_computation.3 | async-start | bytes 3145728 | tf_op jit(solution)/shard_map/all_to_all | solution.py:104
  116.3 1.2 copy-start.2
  117.4 12.8 %all-to-all-start.5 = ((s32[4,1,4]{2,1,0:T(1,128)}), s32[4,1,4]{2,1,0:T(1,128)S(1)}, u32[]{:S(2)}, u32[]{:S(2)}) async-start(s32[4,1,4]{2,1,0:T(1,128)} %bitcast.40), calls=%async_computation.5 | async-start | bytes 4096 | tf_op jit(solution)/shard_map/all_to_all | solution.py:142
  126.2 1.9 %copy-start.6 = (f32[8,128]{1,0:T(8,128)S(1)}, f32[8,128]{1,0:T(8,128)}, u32[]{:S(2)}) copy-start(f32[8,128]{1,0:T(8,128)} %param.24) | copy-start | bytes 12292
  126.2 1.9 %copy-start.7 = (f32[8,128]{1,0:T(8,128)S(1)}, f32[8,128]{1,0:T(8,128)}, u32[]{:S(2)}) copy-start(f32[8,128]{1,0:T(8,128)} %param.25) | copy-start | bytes 12292
  126.3 7.2 %copy-start.12 = (u32[32]{0:T(128)S(1)}, u32[32]{0:T(128)}, u32[]{:S(2)}) copy-start(u32[32]{0:T(128)} %constant.83) | copy-start | bytes 388
  126.3 11.4 %copy-start.9 = (f32[1,1,128]{2,1,0:T(1,128)S(1)}, f32[1,1,128]{2,1,0:T(1,128)}, u32[]{:S(2)}) copy-start(f32[1,1,128]{2,1,0:T(1,128)} %param.30) | copy-start | bytes 1540
  126.3 33.5 %copy-start.11 = (f32[1,8]{1,0:T(1,128)S(1)}, f32[1,8]{1,0:T(1,128)}, u32[]{:S(2)}) copy-start(f32[1,8]{1,0:T(1,128)} %param.31) | copy-start | bytes 100
  130.2 7.1 %all-to-all-start.4 = ((f32[4,4,8]{2,1,0:T(4,128)}), f32[4,4,8]{2,1,0:T(4,128)S(1)}, u32[]{:S(2)}, u32[]{:S(2)}) async-start(f32[4,4,8]{2,1,0:T(4,128)} %bitcast.38), calls=%async_computation.4 | async-start | bytes 16384 | tf_op jit(solution)/shard_map/all_to_all | solution.py:135
where the time goes:
time: 161 us
  blocking collectives  49.9 us (31%)
  waiting for transfers between devices  38.7 us (24%)
  local copies, waits for them, and re-layouts  28.2 us (18%)
  starting transfers between devices  26.7 us (17%)
  between operations  7.51 us (5%)
  other arithmetic  5.32 us (3%)
  matrix products  4.27 us (3%)
    all_to_all x1, waiting for transfers between devices, local(): lax.all_to_all(buffer, 'basin', split_axis=0, concat_axis=0, tiled=True)  35.8 us
    all_gather x1, blocking collectives, entering(): pieces = jax.tree.map(lambda part: lax.all_gather(part, axis), value)  30.4 us
    unnamed x1, blocking collectives  19.5 us
    all_to_all x1, starting transfers between devices, local(): lax.all_to_all(slot_labels, 'basin', split_axis=0, concat_axis=0, tiled=T...  7.28 us
    all_to_all x1, starting transfers between devices, local(): lax.all_to_all(buffer, 'basin', split_axis=0, concat_axis=0, tiled=True)  6.13 us
    slice x1, local copies, waits for them, and re-layouts, land_update(): rain_now = precip[:, sub_step]  4.11 us
    scatter x2, local copies, waits for them, and re-layouts, pack_slots(): buffer = jnp.zeros((peer_count * slot_cap, values.shape[1]), values.dtype...  3.65 us
    reshape x2, local copies, waits for them, and re-layouts, local(): buffer = buffer.reshape(chains, rivers, tile_cap, sub_steps * reaches)  3.63 us
  transfers between devices with their start and end apart: 6, of which 3 were waited for; matrix products, arithmetic and copies ran while one was open for 18% of the time, Pallas kernels for 0%

commit v1 on v0

--- a/solution.py
+++ b/solution.py
@@ -108,12 +108,22 @@
             concat_axis=1,
             tiled=True,
         ),
-        lax.all_to_all(
-            lax.all_to_all(slot_labels, "basin", split_axis=0, concat_axis=0, tiled=True),
-            "band",
-            split_axis=1,
-            concat_axis=1,
-            tiled=True,
+        jnp.concatenate(
+            lax.all_to_all(
+                jnp.stack(
+                    jnp.split(
+                        lax.all_to_all(
+                            slot_labels, "basin", split_axis=0, concat_axis=0, tiled=True
+                        ),
+                        lax.axis_size("band"),
+                        axis=1,
+                    )
+                ),
+                "band",
+                0,
+                0,
+            ),
+            axis=1,
         ),
     )
     received = arrived.reshape(-1, sub_steps * reaches)

time: 161 us -> 161 us (level)
  no operation moved by 1% of the time
where the time goes in v1:
time: 161 us
  blocking collectives  49.9 us (31%)
  waiting for transfers between devices  38.7 us (24%)
  local copies, waits for them, and re-layouts  27.7 us (17%)
  starting transfers between devices  26.7 us (17%)
  between operations  7.51 us (5%)
  other arithmetic  5.93 us (4%)
  matrix products  4.27 us (3%)
    all_to_all x1, waiting for transfers between devices, local(): lax.all_to_all(buffer, 'basin', split_axis=0, concat_axis=0, tiled=True)  35.8 us
    all_gather x1, blocking collectives, entering(): pieces = jax.tree.map(lambda part: lax.all_gather(part, axis), value)  30.4 us
    unnamed x1, blocking collectives  19.5 us
    all_to_all x1, starting transfers between devices, local(): lax.all_to_all(slot_labels, 'basin', split_axis=0, concat_axis=0, tiled=T...  7.28 us
    all_to_all x1, starting transfers between devices, local(): lax.all_to_all(buffer, 'basin', split_axis=0, concat_axis=0, tiled=True)  6.13 us
    slice x1, local copies, waits for them, and re-layouts, land_update(): rain_now = precip[:, sub_step]  4.11 us
    scatter x2, local copies, waits for them, and re-layouts, pack_slots(): buffer = jnp.zeros((peer_count * slot_cap, values.shape[1]), values.dtype...  3.66 us
    reshape x2, local copies, waits for them, and re-layouts, local(): buffer = buffer.reshape(chains, rivers, tile_cap, sub_steps * reaches)  3.64 us
  transfers between devices with their start and end apart: 6, of which 3 were waited for; matrix products, arithmetic and copies ran while one was open for 18% of the time, Pallas kernels for 0%

profile of v1, /device:TPU:0, one launch (start us, length us, event | category | flops | bytes accessed | tf_op | source)
XLA Modules:
  0.0 160.7 jit_solution(16681314854573507074)
XLA Ops:
  0.7 0.9 convert_reduce_fusion
  1.6 0.7 compare_select_fusion
  2.3 1.3 scatter_custom_fusion
  3.7 0.7 reshape.315
  4.4 7.3 %all-to-all-start = ((s32[8,4,12]{2,1,0:T(4,128)}), s32[8,4,12]{2,1,0:T(4,128)S(1)}, u32[]{:S(2)}, u32[]{:S(2)}) async-start(s32[8,4,12]{2,1,0:T(4,128)} %reshape.315), calls=%async_computation | async-start | bytes 32768 | tf_op jit(solution)/shard_map/all_to_all | solution.py:115
  11.7 4.1 %fusion.63 = (f32[192,1,128]{2,1,0:T(1,128)S(1)}, f32[192,1,128]{2,1,0:T(1,128)S(1)}, f32[192,1,128]{2,1,0:T(1,128)S(1)}, f32[192,1,128]{2,1,0:T(1,128)S(1)}, f3...) fusion(f32[192,8,128]{2,1,0:T(8,128)} %param.17), kind=kLoop, calls=%fused_computation.145 | loop fusion | bytes 1572864 | tf_op jit(solution)/shard_map/slice | solution.py:25
  16.0 0.1 bitcast_dynamic-update-slice_fusion.4
  16.4 2.5 %scatter_custom_fusion.1 = f32[384,1024]{1,0:T(8,128)} fusion(s32[192]{0:T(256)S(1)} %compare_select_fusion, f32[8,24,8,128]{3,2,1,0:T(8,128)S(1)} %bitcast.271, f32[]{:T(128)} %constant.60.clone.1), kind=kCustom, calls=%fused_computation.20 | custom fusion | bytes 2359300 | tf_op jit(solution)/shard_map/scatter | solution.py:50
  18.9 1.4 reshape.318
  20.3 2.2 %copy.86 = f32[8,4,12,1024]{3,1,2,0:T(4,128)} copy(f32[8,4,12,1024]{3,2,1,0:T(8,128)S(1)} %reshape.318) | data formatting | bytes 3145728 | tf_op jit(solution)/shard_map/reshape | solution.py:101
  22.5 6.1 %all-to-all-start.2 = ((f32[8,4,12,1024]{3,1,2,0:T(4,128)}), f32[8,4,12,1024]{3,1,2,0:T(4,128)S(1)}, u32[]{:S(2)}, u32[]{:S(2)}) async-start(f32[8,4,12,1024]{3,1,2,0:T(4,128)} %copy.86), calls=%async_computation.2 | async-start | bytes 3145728 | tf_op jit(solution)/shard_map/all_to_all | solution.py:105
  28.7 0.6 pad_add_fusion
  29.3 35.8 %all-to-all-done.2 = f32[8,4,12,1024]{3,1,2,0:T(4,128)S(1)} async-done(((f32[8,4,12,1024]{3,1,2,0:T(4,128)}), f32[8,4,12,1024]{3,1,2,0:T(4,128)S(1)}, u32[]{:S(2)}, u32[]{:S(2)}) %all-to-all-start.2) | async-done | bytes 1572896 | tf_op jit(solution)/shard_map/all_to_all | solution.py:105
  65.1 3.3 %all-to-all-start.1 = ((s32[4,8,1,12]{3,1,2,0:T(8,128)}), s32[4,8,1,12]{3,1,2,0:T(8,128)S(1)}, u32[]{:S(2)}, u32[]{:S(2)}) async-start(s32[4,8,1,12]{3,1,2,0:T(8,128)} %pad_add_fusion), calls=%async_computation.1 | async-start | bytes 32768 | tf_op jit(solution)/shard_map/all_to_all | solution.py:112
  68.4 0.2 convert_reduce_fusion.1
  68.6 2.1 %copy.87 = f32[8,4,12,1024]{3,0,2,1:T(8,128)} copy(f32[8,4,12,1024]{3,1,2,0:T(4,128)S(1)} %all-to-all-done.2) | data formatting | bytes 3145728 | tf_op jit(solution)/shard_map/all_to_all | solution.py:105
  70.7 1.5 all-to-all-done.1
  72.2 3.6 %all-to-all-start.3 = ((f32[8,4,12,1024]{3,0,2,1:T(8,128)}), f32[8,4,12,1024]{3,0,2,1:T(8,128)S(1)}, u32[]{:S(2)}, u32[]{:S(2)}) async-start(f32[8,4,12,1024]{3,0,2,1:T(8,128)} %copy.87), calls=%async_computation.3 | async-start | bytes 3145728 | tf_op jit(solution)/shard_map/all_to_all | solution.py:104
  75.8 0.7 scatter_custom_fusion.3
  76.5 0.7 all_to_all.26
  77.2 0.5 slice.158
  77.7 0.6 slice.129
  84.2 0.7 add_multiply_fusion
  84.9 30.4 %all_gather.7 = f32[8,8,8]{2,1,0:T(8,128)S(1)} all-gather(f32[1,8,8]{2,1,0:T(8,128)S(1)} %add_multiply_fusion), channel_id=1, replica_groups=mesh['basin'=8,'band'=4] {'basin'}, dimensions={0}, use_global_device_ids=true | all-gather | bytes 2304 | tf_op jit(solution)/shard_map/all_gather | solution.py:9
  115.3 0.1 slice_reduce_fusion
  115.4 0.7 add_subtract_fusion
  116.2 0.1 eq.142
  116.3 1.2 copy-done.2
  117.5 3.2 %all-to-all-start.5 = ((s32[4,1,4]{2,1,0:T(1,128)}), s32[4,1,4]{2,1,0:T(1,128)S(1)}, u32[]{:S(2)}, u32[]{:S(2)}) async-start(s32[4,1,4]{2,1,0:T(1,128)} %bitcast.45), calls=%async_computation.5 | async-start | bytes 4096 | tf_op jit(solution)/shard_map/all_to_all | solution.py:152
  120.7 2.4 %copy.88 = f32[8,4,12,1024]{3,2,1,0:T(8,128)S(1)} copy(f32[8,4,12,1024]{3,0,2,1:T(8,128)} %copy-done.2) | data formatting | bytes 3145728 | tf_op jit(solution)/shard_map/all_to_all | solution.py:104
  123.0 1.3 reshape.319
  124.4 1.9 %copy.89 = f32[1024,384]{1,0:T(8,128)S(1)} copy(f32[1024,384]{0,1:T(8,128)} %bitcast.253) | data formatting | bytes 3145728 | tf_op jit(solution)/shard_map/sk,sx->kx/dot_general | solution.py:133
  126.3 0.8 fusion.20
  127.2 0.9 fusion.17
  128.3 0.6 constant_dynamic-update-slice_fusion
  128.9 0.1 copy.98
  129.1 1.2 scatter_custom_fusion.2
  130.2 3.3 %all-to-all-start.4 = ((f32[4,4,8]{2,1,0:T(4,128)}), f32[4,4,8]{2,1,0:T(4,128)S(1)}, u32[]{:S(2)}, u32[]{:S(2)}) async-start(f32[4,4,8]{2,1,0:T(4,128)} %bitcast.43), calls=%async_computation.4 | async-start | bytes 16384 | tf_op jit(solution)/shard_map/all_to_all | solution.py:145
  133.5 0.6 dynamic-slice
  134.8 0.5 broadcast.431
  135.3 0.7 reduce.7
  136.0 1.3 all-to-all-done.4
  137.3 0.2 fusion.22
  137.5 0.2 fusion.49
  137.8 0.2 slice_reduce_fusion.1
  138.0 0.2 dynamic-update-slice
  138.2 19.5 %all-reduce = f32[64]{0:T(128)S(1)} all-reduce(f32[64]{0:T(128)S(1)} %dynamic-update-slice), channel_id=2, replica_groups=mesh['basin'=8,'band'=4] {'basin'}, use_global_device_ids=true, to_apply=%add | all-reduce | flops 64 | bytes 512
  157.8 2.0 %while.16 = (s32[]{:T(128)}, f32[8,8]{1,0:T(8,128)S(1)}, f32[8]{0:T(128)S(1)}, s32[]{:T(128)}, f32[8,8,8]{2,1,0:T(8,128)S(1)}, /*index=5*/f32[8,8]{1,0:T(8,128)S(1)}, s32[]{:T(128)}, s32[]{:T(128)}) while((s32[]{:T(128)}, f32[8,8]{1,0:T(8,128)S(1)}, f32[8]{0:T(128)S(1)}, s32[]{:T(128)}, f32[8,8,8]{2,1,0:T(8,128)S(1)}, ...), condition=%wide.region_7.8_spmd.clone, body=%wide.region_6.7_spmd.clone.sunk | while | flops 7012 | bytes 21460 | solution.py:18
  157.8 0.1 convolution_select_fusion.2
  157.9 0.1 fusion.81
  158.1 0.1 convolution_select_fusion.2
  158.2 0.1 fusion.81
  158.4 0.1 convolution_select_fusion.2
  158.5 0.1 fusion.81
  158.7 0.1 convolution_select_fusion.2
  158.8 0.1 fusion.81
  158.9 0.1 convolution_select_fusion.2
  159.1 0.1 fusion.81
  159.2 0.1 convolution_select_fusion.2
  159.4 0.1 fusion.81
  159.5 0.1 convolution_select_fusion.2
  159.7 0.1 fusion.81
  159.8 0.1 fusion.11
  160.1 0.6 stack.115
  (74 shorter events, 1.1 us)
Async XLA Ops:
  0.6 126.5 %copy-start = (f32[8,128,128]{2,1,0:T(8,128)S(1)}, f32[8,128,128]{2,1,0:T(8,128)}, u32[]{:S(2)}) copy-start(f32[8,128,128]{2,1,0:T(8,128)} %param.23) | copy-start | bytes 1572868
  0.6 15.2 %copy-start.1 = (f32[192,128]{1,0:T(8,128)S(1)}, f32[192,128]{1,0:T(8,128)}, u32[]{:S(2)}) copy-start(f32[192,128]{1,0:T(8,128)} %param.19) | copy-start | bytes 294916
  0.7 15.2 %copy-start.4 = (f32[192,128]{1,0:T(8,128)S(1)}, f32[192,128]{1,0:T(8,128)}, u32[]{:S(2)}) copy-start(f32[192,128]{1,0:T(8,128)} %param.18) | copy-start | bytes 294916
  0.7 15.2 %copy-start.3 = (f32[192,128]{1,0:T(8,128)S(1)}, f32[192,128]{1,0:T(8,128)}, u32[]{:S(2)}) copy-start(f32[192,128]{1,0:T(8,128)} %param.20) | copy-start | bytes 294916
  4.4 18.1 %all-to-all-start = ((s32[8,4,12]{2,1,0:T(4,128)}), s32[8,4,12]{2,1,0:T(4,128)S(1)}, u32[]{:S(2)}, u32[]{:S(2)}) async-start(s32[8,4,12]{2,1,0:T(4,128)} %reshape.315), calls=%async_computation | async-start | bytes 32768 | tf_op jit(solution)/shard_map/all_to_all | solution.py:115
  22.5 45.8 %copy-start.10 = (s32[8]{0:T(128)S(1)}, s32[8]{0:T(128)}, u32[]{:S(2)}) copy-start(s32[8]{0:T(128)} %param.26) | copy-start | bytes 100
  22.5 42.6 %all-to-all-start.2 = ((f32[8,4,12,1024]{3,1,2,0:T(4,128)}), f32[8,4,12,1024]{3,1,2,0:T(4,128)S(1)}, u32[]{:S(2)}, u32[]{:S(2)}) async-start(f32[8,4,12,1024]{3,1,2,0:T(4,128)} %copy.86), calls=%async_computation.2 | async-start | bytes 3145728 | tf_op jit(solution)/shard_map/all_to_all | solution.py:105
  65.1 7.1 %all-to-all-start.1 = ((s32[4,8,1,12]{3,1,2,0:T(8,128)}), s32[4,8,1,12]{3,1,2,0:T(8,128)S(1)}, u32[]{:S(2)}, u32[]{:S(2)}) async-start(s32[4,8,1,12]{3,1,2,0:T(8,128)} %pad_add_fusion), calls=%async_computation.1 | async-start | bytes 32768 | tf_op jit(solution)/shard_map/all_to_all | solution.py:112
  70.7 6.5 %copy-start.5 = (f32[1,1,128,128]{3,2,1,0:T(8,128)S(1)}, f32[1,1,128,128]{3,2,1,0:T(8,128)}, u32[]{:S(2)}) copy-start(f32[1,1,128,128]{3,2,1,0:T(8,128)} %param.28) | copy-start | bytes 196612
  70.7 7.1 %copy-start.8 = (f32[1,1,128]{2,1,0:T(1,128)S(1)}, f32[1,1,128]{2,1,0:T(1,128)}, u32[]{:S(2)}) copy-start(f32[1,1,128]{2,1,0:T(1,128)} %param.29) | copy-start | bytes 1540
  72.2 44.1 %all-to-all-start.3 = ((f32[8,4,12,1024]{3,0,2,1:T(8,128)}), f32[8,4,12,1024]{3,0,2,1:T(8,128)S(1)}, u32[]{:S(2)}, u32[]{:S(2)}) async-start(f32[8,4,12,1024]{3,0,2,1:T(8,128)} %copy.87), calls=%async_computation.3 | async-start | bytes 3145728 | tf_op jit(solution)/shard_map/all_to_all | solution.py:104
  116.3 1.2 copy-start.2
  117.5 12.8 %all-to-all-start.5 = ((s32[4,1,4]{2,1,0:T(1,128)}), s32[4,1,4]{2,1,0:T(1,128)S(1)}, u32[]{:S(2)}, u32[]{:S(2)}) async-start(s32[4,1,4]{2,1,0:T(1,128)} %bitcast.45), calls=%async_computation.5 | async-start | bytes 4096 | tf_op jit(solution)/shard_map/all_to_all | solution.py:152
  126.3 1.9 %copy-start.6 = (f32[8,128]{1,0:T(8,128)S(1)}, f32[8,128]{1,0:T(8,128)}, u32[]{:S(2)}) copy-start(f32[8,128]{1,0:T(8,128)} %param.24) | copy-start | bytes 12292
  126.3 1.9 %copy-start.7 = (f32[8,128]{1,0:T(8,128)S(1)}, f32[8,128]{1,0:T(8,128)}, u32[]{:S(2)}) copy-start(f32[8,128]{1,0:T(8,128)} %param.25) | copy-start | bytes 12292
  126.3 7.2 %copy-start.12 = (u32[32]{0:T(128)S(1)}, u32[32]{0:T(128)}, u32[]{:S(2)}) copy-start(u32[32]{0:T(128)} %constant.83) | copy-start | bytes 388
  126.3 11.4 %copy-start.9 = (f32[1,1,128]{2,1,0:T(1,128)S(1)}, f32[1,1,128]{2,1,0:T(1,128)}, u32[]{:S(2)}) copy-start(f32[1,1,128]{2,1,0:T(1,128)} %param.30) | copy-start | bytes 1540
  126.3 33.5 %copy-start.11 = (f32[1,8]{1,0:T(1,128)S(1)}, f32[1,8]{1,0:T(1,128)}, u32[]{:S(2)}) copy-start(f32[1,8]{1,0:T(1,128)} %param.31) | copy-start | bytes 100
  130.2 7.1 %all-to-all-start.4 = ((f32[4,4,8]{2,1,0:T(4,128)}), f32[4,4,8]{2,1,0:T(4,128)S(1)}, u32[]{:S(2)}, u32[]{:S(2)}) async-start(f32[4,4,8]{2,1,0:T(4,128)} %bitcast.43), calls=%async_computation.4 | async-start | bytes 16384 | tf_op jit(solution)/shard_map/all_to_all | solution.py:145
